TPU v7x, 128 devices: a whole 4x4x4 slice. The times are simulated.
128 devices in a mesh: grp: 8 (over y, core), shard: 16 (over z, x).
Axes of the slice: x: 4, y: 4, z: 4, core: 2. Of those that a mesh axis runs over, the one named last changes fastest.
Arguments:
- tokens: bfloat16 [65536, 2560], P(('grp', 'shard')), may hold values from -6 to 6
- gain: float32 [2560], replicated, may hold values from 0.25 to 1.75
- w_qkv: bfloat16 [2560, 3072], P(None, 'shard'), may hold values from -1 to 1
- prefix_kv: bfloat16 [8, 2048, 512], P('grp', 'shard'), may hold values from -6 to 6
- prefix_owner: int32 [8], P('grp'), may hold values from 0 to 7, as said below
- suffix_len: int32 [8, 16], P('grp', 'shard'), may hold values from 1 to 512, 5120 in all within a row
- slots: int32 [8, 8192], P('grp', 'shard'), may hold values from 0 to 8191, as said below
Outputs:
- attended: bfloat16 [65536, 2560], P(('grp', 'shard'))
Inputs may be any that keep to these rules, and one draw needn't show every extreme that they name: In each group the slots are a permutation of 0 to 8191; in each aligned run of 512 entries the k-th block of 32 entries holds slots k * 512 to (k + 1) * 512 - 1. `suffix_len`: each group's lengths sum to 5120 and one of them equals 512. `prefix_owner`: each entry names one of the 8 caches; several groups may name the same one.
All inputs are finite; a program needn't handle non-finite values.
Results may differ from a plain program's by a relative error of at most 0.0069.
Values may be sent and summed in bfloat16 or wider, within the bound.
No kernel may reach another device: no remote copies, remote signals or barrier semaphores. Data moves between devices by JAX's collectives and lax.ppermute only.
A program may use at most 128 MiB of HBM per device.

v0:
```python
import jax
import jax.numpy as jnp
from jax import lax
from jax.sharding import PartitionSpec as P

H = 10
HD = 256
WINDOW = 2048
SUF = 512
HQ = 2560


def normalize(rows, gain):
    rows32 = rows.astype(jnp.float32)
    factor = lax.rsqrt(jnp.mean(rows32 * rows32, axis=-1, keepdims=True) + 1e-06)
    return (rows32 * factor * gain).astype(jnp.bfloat16)


def attend_request(queries, suffix_kv, prefix, length):
    keys = jnp.concatenate([prefix[:, :HD], suffix_kv[:, :HD]], axis=0)
    values = jnp.concatenate([prefix[:, HD:], suffix_kv[:, HD:]], axis=0)
    span = keys.shape[0]
    prefix_len = prefix.shape[0]
    count = queries.shape[0]
    query_pos = jnp.arange(count, dtype=jnp.int32)[:, None]
    key_pos = jnp.arange(span, dtype=jnp.int32)[None, :]
    visible = (
        (key_pos > prefix_len + query_pos - WINDOW)
        & (key_pos <= prefix_len + query_pos)
        & (key_pos < prefix_len + length)
    )
    heads = queries.reshape(count, H, HD).transpose(1, 0, 2)

    def one_head(head_q):
        scores = jnp.dot(head_q, keys.T, preferred_element_type=jnp.float32) * HD ** (-0.5)
        scores = jnp.where(visible, scores, -1e30)
        top = jnp.max(scores, axis=-1, keepdims=True)
        expd = jnp.exp(scores - top)
        weights = (expd / jnp.sum(expd, axis=-1, keepdims=True)).astype(jnp.bfloat16)
        return jnp.dot(weights, values, preferred_element_type=jnp.float32)

    result = lax.map(one_head, heads).transpose(1, 0, 2).reshape(count, H * HD)
    return jnp.where(query_pos < length, result, 0.0).astype(jnp.bfloat16)


def shards(tokens, gain, w_qkv, prefix_kv, prefix_owner, suffix_len, slots):
    tok_dev = tokens.shape[0]
    order = slots.reshape(tok_dev)
    normed = normalize(tokens, gain)
    projected = jnp.dot(
        normed,
        lax.all_gather(w_qkv, "shard", axis=1, tiled=True),
        preferred_element_type=jnp.float32,
    ).astype(jnp.bfloat16)
    arrived, order = (
        lax.all_to_all(projected, "shard", split_axis=0, concat_axis=0, tiled=True),
        lax.all_to_all(order, "shard", split_axis=0, concat_axis=0, tiled=True),
    )
    first_slot = lax.axis_index("shard") * tok_dev
    placed = jnp.zeros_like(arrived).at[order - first_slot].set(arrived)
    owner = prefix_owner[0]
    sliced = lax.all_gather(prefix_kv, "grp", axis=0, tiled=True)
    chosen = lax.dynamic_index_in_dim(sliced, owner, 0, keepdims=False)
    prefix = lax.all_gather(chosen, "shard", axis=0, tiled=True)
    lengths = suffix_len.reshape(-1)
    req_count = lengths.shape[0]
    blocks = placed.reshape(req_count, SUF, placed.shape[1])
    results = attend_request(blocks[0, :, :HQ], blocks[0, :, HQ:], prefix, lengths[0])
    return results


def solution(mesh):
    return jax.shard_map(
        shards,
        mesh=mesh,
        in_specs=(
            P(("grp", "shard"), None),
            P(),
            P(None, "shard"),
            P("grp", "shard", None),
            P("grp"),
            P("grp", "shard"),
            P("grp", "shard"),
        ),
        out_specs=P(("grp", "shard"), None),
        check_vma=False,
    )
```

profile of v0, /device:TPU:1, one launch (start us, length us, event | category | flops | bytes accessed | tf_op | source)
XLA Modules:
  0.0 314.7 jit_solution(14929914385447946524)
XLA Ops:
  8.5 1.3 reduce.7
  10.6 8.4 %all-to-all-start = ((s32[16,32,1]{1,2,0:T(1,128)}), s32[16,32,1]{1,2,0:T(1,128)S(1)}, u32[]{:S(2)}, u32[]{:S(2)}) async-start(s32[16,32,1]{1,2,0:T(1,128)} %all_to_all.14), calls=%async_computation | async-start | bytes 16384 | tf_op jit(solution)/shard_map/all_to_all | solution.py:57
  19.7 2.4 fusion.11
  22.0 13.9 %all-gather.7.cloned.1.call-done = bf16[8,128,512]{2,1,0:T(8,128)(2,1)} async-done(((bf16[1,128,512]{2,1,0:T(8,128)(2,1)}), bf16[8,128,512]{2,1,0:T(8,128)(2,1)}) %all-gather.7.cloned.1.call-update) | async-done | bytes 1048592 | tf_op jit(solution)/shard_map/all_gather | solution.py:62
  35.9 1.6 constant_dynamic-slice_fusion
  37.5 106.0 %all-gather.5.cloned.1.call-done = bf16[2560,3072]{0,1:T(8,128)(2,1)} async-done(((bf16[2560,192]{0,1:T(8,128)(2,1)}), bf16[2560,3072]{0,1:T(8,128)(2,1)}) %all-gather.5.cloned.1.call-update) | async-done | bytes 15728656 | tf_op jit(solution)/shard_map/all_gather | solution.py:52
  143.5 13.0 %convolution_convert_fusion = bf16[512,3072]{1,0:T(8,128)(2,1)} fusion(bf16[2560,3072]{0,1:T(8,128)(2,1)} %all-gather.5.cloned.1.call-done, bf16[512,2560]{1,0:T(8,128)(2,1)S(1)} %copy-done.3, f32[2560]{0:T(1024)S(1)} %copy-done.5, f32[512]{0:T(512)S(1)} %add_rsqrt_fusion), kind=kOutput, calls=%fused_computation.23 | convolution fusion | flops 8059879424 | bytes 21508096 | tf_op jit(solution)/shard_map/dot_general | solution.py:50
  156.5 5.0 %all-to-all-start.1 = ((bf16[16,32,3072]{2,1,0:T(8,128)(2,1)}), bf16[16,32,3072]{2,1,0:T(8,128)(2,1)S(1)}, u32[]{:S(2)}, u32[]{:S(2)}) async-start(bf16[16,32,3072]{2,1,0:T(8,128)(2,1)} %bitcast.2), calls=%async_computation.1 | async-start | bytes 6291456 | tf_op jit(solution)/shard_map/all_to_all | solution.py:56
  162.3 53.6 %all-gather.9.cloned.1.call-done = bf16[1,2048,512]{2,1,0:T(8,128)(2,1)} async-done(((bf16[1,128,512]{2,1,0:T(8,128)(2,1)}), bf16[1,2048,512]{2,1,0:T(8,128)(2,1)}) %all-gather.9.cloned.1.call-update) | async-done | bytes 2097168 | tf_op jit(solution)/shard_map/all_gather | solution.py:64
  215.9 3.0 fusion.21
  218.9 1.6 copy-done.2
  220.6 7.3 %scatter_custom_fusion = bf16[512,3072]{1,0:T(8,128)(2,1)S(1)} fusion(s32[512]{0:T(512)S(1)} %bitcast.50, bf16[512,3072]{1,0:T(8,128)(2,1)} %bitcast.47, bf16[]{:T(256)} %constant.11.clone.1), kind=kCustom, calls=%fused_computation.26 | custom fusion | bytes 3146240 | tf_op jit(solution)/shard_map/scatter | solution.py:60
  227.9 1.7 slice.24
  230.4 4.5 %copy.20 = bf16[1,512,2560]{1,2,0:T(8,128)(2,1)} copy(bf16[1,512,2560]{2,1,0:T(8,128)(2,1)} %slice.24) | data formatting | bytes 5242880 | tf_op jit(solution)/shard_map/slice | solution.py:68
  235.0 2.3 pad_maximum_fusion
  237.2 65.9 %while.11 = (s32[]{:T(128)}, bf16[10,512,256]{1,2,0:T(8,128)(2,1)}, bf16[10,512,256]{1,2,0:T(8,128)(2,1)}, bf16[2560,256]{1,0:T(8,128)(2,1)S(1)}, bf16[2560,256]...) while((s32[]{:T(128)}, bf16[10,512,256]{1,2,0:T(8,128)(2,1)}, ...), condition=%wide.region_5.6_spmd.clone, body=%wide.region_2.5_spmd.clone.sunk | while | flops 1357904896 | bytes 24395376 | solution.py:42
  237.2 3.2 %fusion.33 = (f32[512]{0:T(512)S(1)}, f32[512,2560]{1,0:T(8,128)S(1)}) fusion(bf16[2560,256]{1,0:T(8,128)(2,1)S(1)} %get-tuple-element.165, bf16[10,512,256]{1,2,0:T(8,128)(2,1)} %get-tuple-element.164, s32[]{:T(128)} %get-tuple-element.154, pred[2560]{0:T(1024)(128)(4,1)S(1)} %get-tuple-element.168, s32[512]{0:T(512)S(1)} %get-tuple-element.167), kind=kOutput, calls=%fused_computation.38.clone.1 | convolution fusion | flops 680263168 | bytes 6822912 | tf_op jit(solution)/shard_map/while/body/eval_jaxpr/dot_general | solution.py:35
  240.5 0.8 fusion.34
  241.8 2.0 fusion.35
  243.8 3.2 %fusion.33 = (f32[512]{0:T(512)S(1)}, f32[512,2560]{1,0:T(8,128)S(1)}) fusion(bf16[2560,256]{1,0:T(8,128)(2,1)S(1)} %get-tuple-element.165, bf16[10,512,256]{1,2,0:T(8,128)(2,1)} %get-tuple-element.164, s32[]{:T(128)} %get-tuple-element.154, pred[2560]{0:T(1024)(128)(4,1)S(1)} %get-tuple-element.168, s32[512]{0:T(512)S(1)} %get-tuple-element.167), kind=kOutput, calls=%fused_computation.38.clone.1 | convolution fusion | flops 680263168 | bytes 6822912 | tf_op jit(solution)/shard_map/while/body/eval_jaxpr/dot_general | solution.py:35
  247.1 0.8 fusion.34
  248.4 2.0 fusion.35
  250.4 3.2 %fusion.33 = (f32[512]{0:T(512)S(1)}, f32[512,2560]{1,0:T(8,128)S(1)}) fusion(bf16[2560,256]{1,0:T(8,128)(2,1)S(1)} %get-tuple-element.165, bf16[10,512,256]{1,2,0:T(8,128)(2,1)} %get-tuple-element.164, s32[]{:T(128)} %get-tuple-element.154, pred[2560]{0:T(1024)(128)(4,1)S(1)} %get-tuple-element.168, s32[512]{0:T(512)S(1)} %get-tuple-element.167), kind=kOutput, calls=%fused_computation.38.clone.1 | convolution fusion | flops 680263168 | bytes 6822912 | tf_op jit(solution)/shard_map/while/body/eval_jaxpr/dot_general | solution.py:35
  253.7 0.8 fusion.34
  255.0 2.0 fusion.35
  257.0 3.2 %fusion.33 = (f32[512]{0:T(512)S(1)}, f32[512,2560]{1,0:T(8,128)S(1)}) fusion(bf16[2560,256]{1,0:T(8,128)(2,1)S(1)} %get-tuple-element.165, bf16[10,512,256]{1,2,0:T(8,128)(2,1)} %get-tuple-element.164, s32[]{:T(128)} %get-tuple-element.154, pred[2560]{0:T(1024)(128)(4,1)S(1)} %get-tuple-element.168, s32[512]{0:T(512)S(1)} %get-tuple-element.167), kind=kOutput, calls=%fused_computation.38.clone.1 | convolution fusion | flops 680263168 | bytes 6822912 | tf_op jit(solution)/shard_map/while/body/eval_jaxpr/dot_general | solution.py:35
  260.3 0.8 fusion.34
  261.6 2.0 fusion.35
  263.6 3.2 %fusion.33 = (f32[512]{0:T(512)S(1)}, f32[512,2560]{1,0:T(8,128)S(1)}) fusion(bf16[2560,256]{1,0:T(8,128)(2,1)S(1)} %get-tuple-element.165, bf16[10,512,256]{1,2,0:T(8,128)(2,1)} %get-tuple-element.164, s32[]{:T(128)} %get-tuple-element.154, pred[2560]{0:T(1024)(128)(4,1)S(1)} %get-tuple-element.168, s32[512]{0:T(512)S(1)} %get-tuple-element.167), kind=kOutput, calls=%fused_computation.38.clone.1 | convolution fusion | flops 680263168 | bytes 6822912 | tf_op jit(solution)/shard_map/while/body/eval_jaxpr/dot_general | solution.py:35
  266.8 0.8 fusion.34
  268.2 2.0 fusion.35
  270.2 3.2 %fusion.33 = (f32[512]{0:T(512)S(1)}, f32[512,2560]{1,0:T(8,128)S(1)}) fusion(bf16[2560,256]{1,0:T(8,128)(2,1)S(1)} %get-tuple-element.165, bf16[10,512,256]{1,2,0:T(8,128)(2,1)} %get-tuple-element.164, s32[]{:T(128)} %get-tuple-element.154, pred[2560]{0:T(1024)(128)(4,1)S(1)} %get-tuple-element.168, s32[512]{0:T(512)S(1)} %get-tuple-element.167), kind=kOutput, calls=%fused_computation.38.clone.1 | convolution fusion | flops 680263168 | bytes 6822912 | tf_op jit(solution)/shard_map/while/body/eval_jaxpr/dot_general | solution.py:35
  273.4 0.8 fusion.34
  274.8 2.0 fusion.35
  276.8 3.2 %fusion.33 = (f32[512]{0:T(512)S(1)}, f32[512,2560]{1,0:T(8,128)S(1)}) fusion(bf16[2560,256]{1,0:T(8,128)(2,1)S(1)} %get-tuple-element.165, bf16[10,512,256]{1,2,0:T(8,128)(2,1)} %get-tuple-element.164, s32[]{:T(128)} %get-tuple-element.154, pred[2560]{0:T(1024)(128)(4,1)S(1)} %get-tuple-element.168, s32[512]{0:T(512)S(1)} %get-tuple-element.167), kind=kOutput, calls=%fused_computation.38.clone.1 | convolution fusion | flops 680263168 | bytes 6822912 | tf_op jit(solution)/shard_map/while/body/eval_jaxpr/dot_general | solution.py:35
  280.0 0.8 fusion.34
  281.3 2.0 fusion.35
  283.4 3.2 %fusion.33 = (f32[512]{0:T(512)S(1)}, f32[512,2560]{1,0:T(8,128)S(1)}) fusion(bf16[2560,256]{1,0:T(8,128)(2,1)S(1)} %get-tuple-element.165, bf16[10,512,256]{1,2,0:T(8,128)(2,1)} %get-tuple-element.164, s32[]{:T(128)} %get-tuple-element.154, pred[2560]{0:T(1024)(128)(4,1)S(1)} %get-tuple-element.168, s32[512]{0:T(512)S(1)} %get-tuple-element.167), kind=kOutput, calls=%fused_computation.38.clone.1 | convolution fusion | flops 680263168 | bytes 6822912 | tf_op jit(solution)/shard_map/while/body/eval_jaxpr/dot_general | solution.py:35
  286.6 0.8 fusion.34
  287.9 2.0 fusion.35
  290.0 3.2 %fusion.33 = (f32[512]{0:T(512)S(1)}, f32[512,2560]{1,0:T(8,128)S(1)}) fusion(bf16[2560,256]{1,0:T(8,128)(2,1)S(1)} %get-tuple-element.165, bf16[10,512,256]{1,2,0:T(8,128)(2,1)} %get-tuple-element.164, s32[]{:T(128)} %get-tuple-element.154, pred[2560]{0:T(1024)(128)(4,1)S(1)} %get-tuple-element.168, s32[512]{0:T(512)S(1)} %get-tuple-element.167), kind=kOutput, calls=%fused_computation.38.clone.1 | convolution fusion | flops 680263168 | bytes 6822912 | tf_op jit(solution)/shard_map/while/body/eval_jaxpr/dot_general | solution.py:35
  293.2 0.8 fusion.34
  294.5 2.0 fusion.35
  296.6 3.2 %fusion.33 = (f32[512]{0:T(512)S(1)}, f32[512,2560]{1,0:T(8,128)S(1)}) fusion(bf16[2560,256]{1,0:T(8,128)(2,1)S(1)} %get-tuple-element.165, bf16[10,512,256]{1,2,0:T(8,128)(2,1)} %get-tuple-element.164, s32[]{:T(128)} %get-tuple-element.154, pred[2560]{0:T(1024)(128)(4,1)S(1)} %get-tuple-element.168, s32[512]{0:T(512)S(1)} %get-tuple-element.167), kind=kOutput, calls=%fused_computation.38.clone.1 | convolution fusion | flops 680263168 | bytes 6822912 | tf_op jit(solution)/shard_map/while/body/eval_jaxpr/dot_general | solution.py:35
  299.8 0.8 fusion.34
  301.1 2.0 fusion.35
  303.2 2.2 fusion.14
  305.4 2.8 copy.23
  (49 shorter events, 8.5 us)
Async XLA Ops:
  6.5 137.0 %copy-start.3 = (bf16[512,2560]{1,0:T(8,128)(2,1)S(1)}, bf16[512,2560]{1,0:T(8,128)(2,1)}, u32[]{:S(2)}) copy-start(bf16[512,2560]{1,0:T(8,128)(2,1)} %param.9) | copy-start | bytes 7864324
  6.5 137.0 %copy-start.5 = (f32[2560]{0:T(1024)S(1)}, f32[2560]{0:T(1024)}, u32[]{:S(2)}) copy-start(f32[2560]{0:T(1024)} %param.10) | copy-start | bytes 30724
  6.5 29.4 %all-gather.7.cloned.1.call-start = ((), (), s32[]{:S(2)}) async-start(), calls=%async_computation.3 | async-start | bytes 1179648 | tf_op jit(solution)/shard_map/all_gather | solution.py:62
  7.3 136.2 %all-gather.5.cloned.1.call-start = ((), (), s32[]{:S(2)}) async-start(), calls=%async_computation.2 | async-start | bytes 16711680 | tf_op jit(solution)/shard_map/all_gather | solution.py:52
  10.6 145.9 %all-to-all-start = ((s32[16,32,1]{1,2,0:T(1,128)}), s32[16,32,1]{1,2,0:T(1,128)S(1)}, u32[]{:S(2)}, u32[]{:S(2)}) async-start(s32[16,32,1]{1,2,0:T(1,128)} %all_to_all.14), calls=%async_computation | async-start | bytes 16384 | tf_op jit(solution)/shard_map/all_to_all | solution.py:57
  19.0 196.9 %all-gather.9.cloned.1.call-start = ((), (), s32[]{:S(2)}) async-start(), calls=%async_computation.4 | async-start | bytes 2228224 | tf_op jit(solution)/shard_map/all_gather | solution.py:64
  156.5 62.4 %all-to-all-start.1 = ((bf16[16,32,3072]{2,1,0:T(8,128)(2,1)}), bf16[16,32,3072]{2,1,0:T(8,128)(2,1)S(1)}, u32[]{:S(2)}, u32[]{:S(2)}) async-start(bf16[16,32,3072]{2,1,0:T(8,128)(2,1)} %bitcast.2), calls=%async_computation.1 | async-start | bytes 6291456 | tf_op jit(solution)/shard_map/all_to_all | solution.py:56
  218.9 1.6 copy-start.2
  230.4 4.5 %copy-start = (bf16[2048,256]{1,0:T(8,128)(2,1)S(1)}, bf16[2048,256]{1,0:T(8,128)(2,1)}, u32[]{:S(2)}) copy-start(bf16[2048,256]{1,0:T(8,128)(2,1)} %get-tuple-element.93) | copy-start | bytes 3145732
  230.4 4.5 %copy-start.1 = (bf16[2048,256]{1,0:T(8,128)(2,1)S(1)}, bf16[2048,256]{1,0:T(8,128)(2,1)}, u32[]{:S(2)}) copy-start(bf16[2048,256]{1,0:T(8,128)(2,1)} %get-tuple-element.94) | copy-start | bytes 3145732
  240.5 1.3 copy-start.4
  247.1 1.3 copy-start.4
  253.7 1.3 copy-start.4
  260.2 1.3 copy-start.4
  266.8 1.3 copy-start.4
  273.4 1.3 copy-start.4
  280.0 1.3 copy-start.4
  286.6 1.3 copy-start.4
  293.2 1.3 copy-start.4
  299.8 1.3 copy-start.4
Sparse Core Ops, SparseCore 0:
  9.0 26.8 all-gather.6
  38.1 105.3 all-gather.4
  145.6 70.2 all-gather.8
where the time goes:
time: 316 us; the launch traced here: 315 us
  waiting for transfers between devices  175 us (55%)
  matrix products  65.7 us (21%)
  local copies, waits for them, and re-layouts  29.4 us (9%)
  other arithmetic  16.6 us (5%)
  between operations  14.5 us (5%)
  starting transfers between devices  13.5 us (4%)
    all_gather x1, waiting for transfers between devices, shards(): lax.all_gather(w_qkv, 'shard', axis=1, tiled=True)  106 us
    all_gather x1, waiting for transfers between devices, shards(): prefix = lax.all_gather(chosen, 'shard', axis=0, tiled=True)  53.6 us
    dot_general x10, matrix products, one_head(): jnp.dot(head_q, keys.T, preferred_element_type=jnp.float32) * HD ** (-0.5)  32.5 us
    dot_general x10, matrix products, one_head(): return jnp.dot(weights, values, preferred_element_type=jnp.float32)  20.2 us
    all_gather x1, waiting for transfers between devices, shards(): sliced = lax.all_gather(prefix_kv, 'grp', axis=0, tiled=True)  13.9 us
    dot_general x1, matrix products, shards(): jnp.dot(normed, lax.all_gather(w_qkv, 'shard', axis=1, tiled=True), prefe...  13 us
    all_to_all x1, starting transfers between devices, shards(): lax.all_to_all(order, 'shard', split_axis=0, concat_axis=0, tiled=True)  8.42 us
    reduce_sum x10, other arithmetic, one_head(): jnp.sum(expd, axis=-1, keepdims=True)  8.39 us
  transfers between devices with their start and end apart: 5, of which 3 were waited for; matrix products, arithmetic and copies ran while one was open for 7% of the time, Pallas kernels for 0%

commit v1 on v0

--- a/solution.py
+++ b/solution.py
@@ -8,6 +8,12 @@
 WINDOW = 2048
 SUF = 512
 HQ = 2560
+
+
+def in_order(parts, dim):
+    parts = jnp.moveaxis(parts, 0, dim)
+    lengths = parts.shape
+    return parts.reshape(*lengths[:dim], lengths[dim] * lengths[dim + 1], *lengths[dim + 2 :])
 
 
 def normalize(rows, gain):
@@ -59,7 +65,19 @@
     first_slot = lax.axis_index("shard") * tok_dev
     placed = jnp.zeros_like(arrived).at[order - first_slot].set(arrived)
     owner = prefix_owner[0]
-    sliced = lax.all_gather(prefix_kv, "grp", axis=0, tiled=True)
+    devices = lax.axis_size("grp")
+    pairs = [(i, (i + 1) % devices) for i in range(devices)]
+    back = [(b, a) for a, b in pairs]
+    lower, upper = ([], [])
+    for lap in range(devices - 1):
+        if lap % 2 == 0:
+            lower.append(lax.ppermute(lower[-1] if lower else prefix_kv, "grp", pairs))
+        else:
+            upper.append(lax.ppermute(upper[-1] if upper else prefix_kv, "grp", back))
+    blocks_2 = jnp.stack([*lower[::-1], prefix_kv, *upper])
+    shift = lax.axis_index("grp") - len(lower)
+    blocks_2 = blocks_2[(jnp.arange(devices) - shift) % devices]
+    sliced = in_order(blocks_2, 0)
     chosen = lax.dynamic_index_in_dim(sliced, owner, 0, keepdims=False)
     prefix = lax.all_gather(chosen, "shard", axis=0, tiled=True)
     lengths = suffix_len.reshape(-1)

time: 316 us -> 290 us (0.918)
  waiting for transfers between devices: 175 us -> 129 us
  starting transfers between devices: 13.5 us -> 25.1 us
  local copies, waits for them, and re-layouts: 29.4 us -> 37.6 us
    all_gather x1, waiting for transfers between devices: 106 us -> 73.5 us  [shards(): lax.all_gather(w_qkv, 'shard', axis=1, tiled=True)]
    all_gather x1 -> x0, waiting for transfers between devices: 13.9 us -> none  [shards(): sliced = lax.all_gather(prefix_kv, 'grp', axis=0, tiled=True)]
    ppermute x0 -> x7, starting transfers between devices: none -> 12.5 us  [the longest x4 8.74 us: shards(): lower.append(lax.ppermute(lower[-1] if lower else prefix_kv, 'grp', pairs))]
    unnamed x11 -> x23, local copies, waits for them, and re-layouts: 2.17 us -> 8.36 us
  transfers between devices with their start and end apart: 5 -> 11, of which waited for: 3 -> 3; matrix products, arithmetic and copies ran while one was open for 7% -> 11% of each run, Pallas kernels for 0% -> 0%
where the time goes in v1:
time: 290 us; the launch traced here: 289 us
  waiting for transfers between devices  129 us (44%)
  matrix products  65.7 us (23%)
  local copies, waits for them, and re-layouts  37.6 us (13%)
  starting transfers between devices  25.1 us (9%)
  other arithmetic  17.1 us (6%)
  between operations  14.8 us (5%)
    all_gather x1, waiting for transfers between devices, shards(): lax.all_gather(w_qkv, 'shard', axis=1, tiled=True)  73.5 us
    all_gather x1, waiting for transfers between devices, shards(): prefix = lax.all_gather(chosen, 'shard', axis=0, tiled=True)  53.5 us
    dot_general x10, matrix products, one_head(): jnp.dot(head_q, keys.T, preferred_element_type=jnp.float32) * HD ** (-0.5)  32.4 us
    dot_general x10, matrix products, one_head(): return jnp.dot(weights, values, preferred_element_type=jnp.float32)  20.2 us
    dot_general x1, matrix products, shards(): jnp.dot(normed, lax.all_gather(w_qkv, 'shard', axis=1, tiled=True), prefe...  13 us
    ppermute x4, starting transfers between devices, shards(): lower.append(lax.ppermute(lower[-1] if lower else prefix_kv, 'grp', pairs))  8.74 us
    reduce_sum x10, other arithmetic, one_head(): jnp.sum(expd, axis=-1, keepdims=True)  8.39 us
    unnamed x23, local copies, waits for them, and re-layouts  8.36 us
  transfers between devices with their start and end apart: 11, of which 3 were waited for; matrix products, arithmetic and copies ran while one was open for 11% of the time, Pallas kernels for 0%

profile of v1, /device:TPU:1, one launch (start us, length us, event | category | flops | bytes accessed | tf_op | source)
XLA Modules:
  0.0 289.0 jit_solution(17334438274319289056)
XLA Ops:
  7.3 2.7 collective-permute-start
  10.5 1.3 reduce.7
  12.5 7.6 %all-to-all-start = ((s32[16,32,1]{1,2,0:T(1,128)}), s32[16,32,1]{1,2,0:T(1,128)S(1)}, u32[]{:S(2)}, u32[]{:S(2)}) async-start(s32[16,32,1]{1,2,0:T(1,128)} %all_to_all.14), calls=%async_computation | async-start | bytes 16384 | tf_op jit(solution)/shard_map/all_to_all | solution.py:63
  20.2 2.0 collective-permute-start.1
  22.2 2.7 fusion.11
  24.9 1.7 collective-permute-start.2
  26.6 1.3 collective-permute-start.5
  28.7 2.3 collective-permute-start.3
  32.8 2.5 collective-permute-start.6
  40.6 2.8 gather_fusion
  43.4 1.5 constant_dynamic-slice_fusion
  45.0 73.5 %all-gather.5.cloned.1.call-done = bf16[2560,3072]{0,1:T(8,128)(2,1)} async-done(((bf16[2560,192]{0,1:T(8,128)(2,1)}), bf16[2560,3072]{0,1:T(8,128)(2,1)}) %all-gather.5.cloned.1.call-update) | async-done | bytes 15728656 | tf_op jit(solution)/shard_map/all_gather | solution.py:58
  118.5 13.0 %convolution_convert_fusion = bf16[512,3072]{1,0:T(8,128)(2,1)} fusion(bf16[2560,3072]{0,1:T(8,128)(2,1)} %all-gather.5.cloned.1.call-done, bf16[512,2560]{1,0:T(8,128)(2,1)S(1)} %copy-done.3, f32[2560]{0:T(1024)S(1)} %copy-done.7, f32[512]{0:T(512)S(1)} %add_rsqrt_fusion), kind=kOutput, calls=%fused_computation.24 | convolution fusion | flops 8059879424 | bytes 21508096 | tf_op jit(solution)/shard_map/dot_general | solution.py:56
  131.5 5.0 %all-to-all-start.1 = ((bf16[16,32,3072]{2,1,0:T(8,128)(2,1)}), bf16[16,32,3072]{2,1,0:T(8,128)(2,1)S(1)}, u32[]{:S(2)}, u32[]{:S(2)}) async-start(bf16[16,32,3072]{2,1,0:T(8,128)(2,1)} %bitcast.2), calls=%async_computation.1 | async-start | bytes 6291456 | tf_op jit(solution)/shard_map/all_to_all | solution.py:62
  137.4 53.5 %all-gather.7.cloned.1.call-done = bf16[1,2048,512]{2,1,0:T(8,128)(2,1)} async-done(((bf16[1,128,512]{2,1,0:T(8,128)(2,1)}), bf16[1,2048,512]{2,1,0:T(8,128)(2,1)}) %all-gather.7.cloned.1.call-update) | async-done | bytes 2097168 | tf_op jit(solution)/shard_map/all_gather | solution.py:82
  190.9 3.0 %fusion.23 = (bf16[2048,256]{1,0:T(8,128)(2,1)}, bf16[2048,256]{1,0:T(8,128)(2,1)}) fusion(bf16[2048,512]{1,0:T(8,128)(2,1)} %bitcast.69), kind=kLoop, calls=%fused_computation.55 | loop fusion | bytes 4194304 | tf_op jit(solution)/shard_map/slice | solution.py:27
  193.9 1.6 copy-done.2
  195.6 7.3 %scatter_custom_fusion = bf16[512,3072]{1,0:T(8,128)(2,1)S(1)} fusion(s32[512]{0:T(512)S(1)} %bitcast.70, bf16[512,3072]{1,0:T(8,128)(2,1)} %bitcast.67, bf16[]{:T(256)} %constant.35.clone.1), kind=kCustom, calls=%fused_computation.27 | custom fusion | bytes 3146240 | tf_op jit(solution)/shard_map/scatter | solution.py:66
  203.7 1.7 slice.26
  205.4 4.6 %copy.20 = bf16[1,512,2560]{1,2,0:T(8,128)(2,1)} copy(bf16[1,512,2560]{2,1,0:T(8,128)(2,1)} %slice.26) | data formatting | bytes 5242880 | tf_op jit(solution)/shard_map/slice | solution.py:86
  210.0 1.2 pad_maximum_fusion
  211.2 65.9 %while.11 = (s32[]{:T(128)}, bf16[10,512,256]{1,2,0:T(8,128)(2,1)}, bf16[10,512,256]{1,2,0:T(8,128)(2,1)}, bf16[2560,256]{1,0:T(8,128)(2,1)S(1)}, bf16[2560,256]...) while((s32[]{:T(128)}, bf16[10,512,256]{1,2,0:T(8,128)(2,1)}, ...), condition=%wide.region_5.6_spmd.clone, body=%wide.region_2.5_spmd.clone.sunk | while | flops 1357904896 | bytes 24394368 | solution.py:48
  211.3 3.2 %fusion.35 = (f32[512]{0:T(512)S(1)}, f32[512,2560]{1,0:T(8,128)S(1)}) fusion(bf16[2560,256]{1,0:T(8,128)(2,1)S(1)} %get-tuple-element.165, bf16[10,512,256]{1,2,0:T(8,128)(2,1)} %get-tuple-element.164, s32[]{:T(128)S(6)} %copy.38, pred[2560]{0:T(1024)(128)(4,1)S(1)} %get-tuple-element.168, s32[512]{0:T(512)S(1)} %get-tuple-element.167), kind=kOutput, calls=%fused_computation.54.clone.1 | convolution fusion | flops 680263168 | bytes 6822404 | tf_op jit(solution)/shard_map/while/body/eval_jaxpr/dot_general | solution.py:41
  214.5 0.8 fusion.36
  215.8 2.0 fusion.37
  217.8 3.2 %fusion.35 = (f32[512]{0:T(512)S(1)}, f32[512,2560]{1,0:T(8,128)S(1)}) fusion(bf16[2560,256]{1,0:T(8,128)(2,1)S(1)} %get-tuple-element.165, bf16[10,512,256]{1,2,0:T(8,128)(2,1)} %get-tuple-element.164, s32[]{:T(128)S(6)} %copy.38, pred[2560]{0:T(1024)(128)(4,1)S(1)} %get-tuple-element.168, s32[512]{0:T(512)S(1)} %get-tuple-element.167), kind=kOutput, calls=%fused_computation.54.clone.1 | convolution fusion | flops 680263168 | bytes 6822404 | tf_op jit(solution)/shard_map/while/body/eval_jaxpr/dot_general | solution.py:41
  222.4 2.0 fusion.37
  224.4 3.2 %fusion.35 = (f32[512]{0:T(512)S(1)}, f32[512,2560]{1,0:T(8,128)S(1)}) fusion(bf16[2560,256]{1,0:T(8,128)(2,1)S(1)} %get-tuple-element.165, bf16[10,512,256]{1,2,0:T(8,128)(2,1)} %get-tuple-element.164, s32[]{:T(128)S(6)} %copy.38, pred[2560]{0:T(1024)(128)(4,1)S(1)} %get-tuple-element.168, s32[512]{0:T(512)S(1)} %get-tuple-element.167), kind=kOutput, calls=%fused_computation.54.clone.1 | convolution fusion | flops 680263168 | bytes 6822404 | tf_op jit(solution)/shard_map/while/body/eval_jaxpr/dot_general | solution.py:41
  229.0 2.0 fusion.37
  231.0 3.2 %fusion.35 = (f32[512]{0:T(512)S(1)}, f32[512,2560]{1,0:T(8,128)S(1)}) fusion(bf16[2560,256]{1,0:T(8,128)(2,1)S(1)} %get-tuple-element.165, bf16[10,512,256]{1,2,0:T(8,128)(2,1)} %get-tuple-element.164, s32[]{:T(128)S(6)} %copy.38, pred[2560]{0:T(1024)(128)(4,1)S(1)} %get-tuple-element.168, s32[512]{0:T(512)S(1)} %get-tuple-element.167), kind=kOutput, calls=%fused_computation.54.clone.1 | convolution fusion | flops 680263168 | bytes 6822404 | tf_op jit(solution)/shard_map/while/body/eval_jaxpr/dot_general | solution.py:41
  235.6 2.0 fusion.37
  237.6 3.2 %fusion.35 = (f32[512]{0:T(512)S(1)}, f32[512,2560]{1,0:T(8,128)S(1)}) fusion(bf16[2560,256]{1,0:T(8,128)(2,1)S(1)} %get-tuple-element.165, bf16[10,512,256]{1,2,0:T(8,128)(2,1)} %get-tuple-element.164, s32[]{:T(128)S(6)} %copy.38, pred[2560]{0:T(1024)(128)(4,1)S(1)} %get-tuple-element.168, s32[512]{0:T(512)S(1)} %get-tuple-element.167), kind=kOutput, calls=%fused_computation.54.clone.1 | convolution fusion | flops 680263168 | bytes 6822404 | tf_op jit(solution)/shard_map/while/body/eval_jaxpr/dot_general | solution.py:41
  240.9 0.8 fusion.36
  242.2 2.0 fusion.37
  244.2 3.2 %fusion.35 = (f32[512]{0:T(512)S(1)}, f32[512,2560]{1,0:T(8,128)S(1)}) fusion(bf16[2560,256]{1,0:T(8,128)(2,1)S(1)} %get-tuple-element.165, bf16[10,512,256]{1,2,0:T(8,128)(2,1)} %get-tuple-element.164, s32[]{:T(128)S(6)} %copy.38, pred[2560]{0:T(1024)(128)(4,1)S(1)} %get-tuple-element.168, s32[512]{0:T(512)S(1)} %get-tuple-element.167), kind=kOutput, calls=%fused_computation.54.clone.1 | convolution fusion | flops 680263168 | bytes 6822404 | tf_op jit(solution)/shard_map/while/body/eval_jaxpr/dot_general | solution.py:41
  248.8 2.0 fusion.37
  250.8 3.2 %fusion.35 = (f32[512]{0:T(512)S(1)}, f32[512,2560]{1,0:T(8,128)S(1)}) fusion(bf16[2560,256]{1,0:T(8,128)(2,1)S(1)} %get-tuple-element.165, bf16[10,512,256]{1,2,0:T(8,128)(2,1)} %get-tuple-element.164, s32[]{:T(128)S(6)} %copy.38, pred[2560]{0:T(1024)(128)(4,1)S(1)} %get-tuple-element.168, s32[512]{0:T(512)S(1)} %get-tuple-element.167), kind=kOutput, calls=%fused_computation.54.clone.1 | convolution fusion | flops 680263168 | bytes 6822404 | tf_op jit(solution)/shard_map/while/body/eval_jaxpr/dot_general | solution.py:41
  254.1 0.8 fusion.36
  255.4 2.0 fusion.37
  257.4 3.2 %fusion.35 = (f32[512]{0:T(512)S(1)}, f32[512,2560]{1,0:T(8,128)S(1)}) fusion(bf16[2560,256]{1,0:T(8,128)(2,1)S(1)} %get-tuple-element.165, bf16[10,512,256]{1,2,0:T(8,128)(2,1)} %get-tuple-element.164, s32[]{:T(128)S(6)} %copy.38, pred[2560]{0:T(1024)(128)(4,1)S(1)} %get-tuple-element.168, s32[512]{0:T(512)S(1)} %get-tuple-element.167), kind=kOutput, calls=%fused_computation.54.clone.1 | convolution fusion | flops 680263168 | bytes 6822404 | tf_op jit(solution)/shard_map/while/body/eval_jaxpr/dot_general | solution.py:41
  262.0 2.0 fusion.37
  264.0 3.2 %fusion.35 = (f32[512]{0:T(512)S(1)}, f32[512,2560]{1,0:T(8,128)S(1)}) fusion(bf16[2560,256]{1,0:T(8,128)(2,1)S(1)} %get-tuple-element.165, bf16[10,512,256]{1,2,0:T(8,128)(2,1)} %get-tuple-element.164, s32[]{:T(128)S(6)} %copy.38, pred[2560]{0:T(1024)(128)(4,1)S(1)} %get-tuple-element.168, s32[512]{0:T(512)S(1)} %get-tuple-element.167), kind=kOutput, calls=%fused_computation.54.clone.1 | convolution fusion | flops 680263168 | bytes 6822404 | tf_op jit(solution)/shard_map/while/body/eval_jaxpr/dot_general | solution.py:41
  267.2 0.8 fusion.36
  268.6 2.0 fusion.37
  270.6 3.2 %fusion.35 = (f32[512]{0:T(512)S(1)}, f32[512,2560]{1,0:T(8,128)S(1)}) fusion(bf16[2560,256]{1,0:T(8,128)(2,1)S(1)} %get-tuple-element.165, bf16[10,512,256]{1,2,0:T(8,128)(2,1)} %get-tuple-element.164, s32[]{:T(128)S(6)} %copy.38, pred[2560]{0:T(1024)(128)(4,1)S(1)} %get-tuple-element.168, s32[512]{0:T(512)S(1)} %get-tuple-element.167), kind=kOutput, calls=%fused_computation.54.clone.1 | convolution fusion | flops 680263168 | bytes 6822404 | tf_op jit(solution)/shard_map/while/body/eval_jaxpr/dot_general | solution.py:41
  275.2 2.0 fusion.37
  277.2 2.2 fusion.14
  279.4 2.8 copy.23
  (75 shorter events, 20.1 us)
Async XLA Ops:
  6.5 31.4 %copy-start.6 = (bf16[1,128,512]{2,1,0:T(8,128)(2,1)S(1)}, bf16[1,128,512]{2,1,0:T(8,128)(2,1)}, u32[]{:S(2)}) copy-start(bf16[1,128,512]{2,1,0:T(8,128)(2,1)} %param.12) | copy-start | bytes 393220
  6.5 112.0 %all-gather.5.cloned.1.call-start = ((), (), s32[]{:S(2)}) async-start(), calls=%async_computation.2 | async-start | bytes 16711680 | tf_op jit(solution)/shard_map/all_gather | solution.py:58
  7.3 12.9 %collective-permute-start = (bf16[1,128,512]{2,1,0:T(8,128)(2,1)}, bf16[1,128,512]{2,1,0:T(8,128)(2,1)S(1)}, u32[]{:S(2)}, u32[]{:S(2)}) collective-permute-start(bf16[1,128,512]{2,1,0:T(8,128)(2,1)} %param.12), channel_id=1, source_target_pairs={{0,16},{16,32},{32,48},{48,64},{64,80},{80,96},{96,112},{112,0},{1... | collective-permute-start | bytes 393224 | tf_op jit(solution)/shard_map/ppermute | solution.py:74
  9.9 16.6 %collective-permute-start.4 = (bf16[1,128,512]{2,1,0:T(8,128)(2,1)}, bf16[1,128,512]{2,1,0:T(8,128)(2,1)S(1)}, u32[]{:S(2)}, u32[]{:S(2)}) collective-permute-start(bf16[1,128,512]{2,1,0:T(8,128)(2,1)} %param.12), channel_id=1, source_target_pairs={{16,0},{32,16},{48,32},{64,48},{80,64},{96,80},{112,96},{0,112},{1... | collective-permute-start | bytes 393224 | tf_op jit(solution)/shard_map/ppermute | solution.py:76
  12.5 119.1 %all-to-all-start = ((s32[16,32,1]{1,2,0:T(1,128)}), s32[16,32,1]{1,2,0:T(1,128)S(1)}, u32[]{:S(2)}, u32[]{:S(2)}) async-start(s32[16,32,1]{1,2,0:T(1,128)} %all_to_all.14), calls=%async_computation | async-start | bytes 16384 | tf_op jit(solution)/shard_map/all_to_all | solution.py:63
  20.1 170.8 %all-gather.7.cloned.1.call-start = ((), (), s32[]{:S(2)}) async-start(), calls=%async_computation.3 | async-start | bytes 2228224 | tf_op jit(solution)/shard_map/all_gather | solution.py:82
  20.2 4.7 %collective-permute-start.1 = (bf16[1,128,512]{2,1,0:T(8,128)(2,1)S(1)}, bf16[1,128,512]{2,1,0:T(8,128)(2,1)S(1)}, u32[]{:S(2)}, u32[]{:S(2)}) collective-permute-start(bf16[1,128,512]{2,1,0:T(8,128)(2,1)S(1)} %collective-permute-done), channel_id=1, source_target_pairs={{0,16},{16,32},{32,48},{48,64},{64,80},{80,96},{96,112},{112,0},{1... | collective-permute-start | bytes 393224 | tf_op jit(solution)/shard_map/ppermute | solution.py:74
  24.9 93.7 %copy-start.3 = (bf16[512,2560]{1,0:T(8,128)(2,1)S(1)}, bf16[512,2560]{1,0:T(8,128)(2,1)}, u32[]{:S(2)}) copy-start(bf16[512,2560]{1,0:T(8,128)(2,1)} %param.9) | copy-start | bytes 7864324
  24.9 3.8 %collective-permute-start.2 = (bf16[1,128,512]{2,1,0:T(8,128)(2,1)S(1)}, bf16[1,128,512]{2,1,0:T(8,128)(2,1)S(1)}, u32[]{:S(2)}, u32[]{:S(2)}) collective-permute-start(bf16[1,128,512]{2,1,0:T(8,128)(2,1)S(1)} %collective-permute-done.1), channel_id=1, source_target_pairs={{0,16},{16,32},{32,48},{48,64},{64,80},{80,96},{96,112},{112,0},{1... | collective-permute-start | bytes 393224 | tf_op jit(solution)/shard_map/ppermute | solution.py:74
  26.6 6.2 %collective-permute-start.5 = (bf16[1,128,512]{2,1,0:T(8,128)(2,1)S(1)}, bf16[1,128,512]{2,1,0:T(8,128)(2,1)S(1)}, u32[]{:S(2)}, u32[]{:S(2)}) collective-permute-start(bf16[1,128,512]{2,1,0:T(8,128)(2,1)S(1)} %collective-permute-done.4), channel_id=1, source_target_pairs={{16,0},{32,16},{48,32},{64,48},{80,64},{96,80},{112,96},{0,112},{1... | collective-permute-start | bytes 393224 | tf_op jit(solution)/shard_map/ppermute | solution.py:76
  28.7 6.6 %collective-permute-start.3 = (bf16[1,128,512]{2,1,0:T(8,128)(2,1)S(1)}, bf16[1,128,512]{2,1,0:T(8,128)(2,1)S(1)}, u32[]{:S(2)}, u32[]{:S(2)}) collective-permute-start(bf16[1,128,512]{2,1,0:T(8,128)(2,1)S(1)} %collective-permute-done.2), channel_id=1, source_target_pairs={{0,16},{16,32},{32,48},{48,64},{64,80},{80,96},{96,112},{112,0},{1... | collective-permute-start | bytes 393224 | tf_op jit(solution)/shard_map/ppermute | solution.py:74
  32.8 7.1 %collective-permute-start.6 = (bf16[1,128,512]{2,1,0:T(8,128)(2,1)S(1)}, bf16[1,128,512]{2,1,0:T(8,128)(2,1)S(1)}, u32[]{:S(2)}, u32[]{:S(2)}) collective-permute-start(bf16[1,128,512]{2,1,0:T(8,128)(2,1)S(1)} %collective-permute-done.5), channel_id=1, source_target_pairs={{16,0},{32,16},{48,32},{64,48},{80,64},{96,80},{112,96},{0,112},{1... | collective-permute-start | bytes 393224 | tf_op jit(solution)/shard_map/ppermute | solution.py:76
  35.9 82.6 %copy-start.7 = (f32[2560]{0:T(1024)S(1)}, f32[2560]{0:T(1024)}, u32[]{:S(2)}) copy-start(f32[2560]{0:T(1024)} %param.10) | copy-start | bytes 30724
  131.5 62.4 %all-to-all-start.1 = ((bf16[16,32,3072]{2,1,0:T(8,128)(2,1)}), bf16[16,32,3072]{2,1,0:T(8,128)(2,1)S(1)}, u32[]{:S(2)}, u32[]{:S(2)}) async-start(bf16[16,32,3072]{2,1,0:T(8,128)(2,1)} %bitcast.2), calls=%async_computation.1 | async-start | bytes 6291456 | tf_op jit(solution)/shard_map/all_to_all | solution.py:62
  193.9 1.6 copy-start.2
  205.4 4.6 %copy-start.4 = (bf16[512,512]{1,0:T(8,128)(2,1)S(1)}, bf16[512,512]{1,0:T(8,128)(2,1)}, u32[]{:S(2)}) copy-start(bf16[512,512]{1,0:T(8,128)(2,1)} %slice_bitcast_fusion) | copy-start | bytes 1572868
  205.4 4.6 %copy-start = (bf16[2048,256]{1,0:T(8,128)(2,1)S(1)}, bf16[2048,256]{1,0:T(8,128)(2,1)}, u32[]{:S(2)}) copy-start(bf16[2048,256]{1,0:T(8,128)(2,1)} %get-tuple-element.93) | copy-start | bytes 3145732
  205.4 4.6 %copy-start.1 = (bf16[2048,256]{1,0:T(8,128)(2,1)S(1)}, bf16[2048,256]{1,0:T(8,128)(2,1)}, u32[]{:S(2)}) copy-start(bf16[2048,256]{1,0:T(8,128)(2,1)} %get-tuple-element.94) | copy-start | bytes 3145732
  214.5 1.3 copy-start.5
  221.1 1.3 copy-start.5
  227.7 1.3 copy-start.5
  234.3 1.3 copy-start.5
  240.9 1.3 copy-start.5
  247.5 1.3 copy-start.5
  254.1 1.3 copy-start.5
  260.6 1.3 copy-start.5
  267.2 1.3 copy-start.5
  273.8 1.3 copy-start.5
Sparse Core Ops, SparseCore 0:
  9.5 108.9 all-gather.4
  120.7 70.1 all-gather.6
